TPU v7x, 512 devices: a whole 4x4x16 slice. The times are simulated.
512 devices in a mesh: pts: 128 (over z, x, core), grp: 4 (over y).
Axes of the slice: x: 4, y: 4, z: 16, core: 2. Of those that a mesh axis runs over, the one named last changes fastest.
Arguments:
- jac_cam: float32 [12, 4, 524288], P(None, None, ('pts', 'grp')), may hold values from -2 to 2
- jac_pt: float32 [6, 4, 524288], P(None, None, ('pts', 'grp')), may hold values from -7 to 7
- resid: float32 [2, 4, 524288], P(None, None, ('pts', 'grp')), may hold values from -6 to 6
- obs_slot: int32 [4, 524288], P(None, ('pts', 'grp')), may hold values from 0 to 2047, as said below
- requests: int32 [4, 4, 4, 16384], P('grp', None, None, 'pts'), may hold values from -1 to 255, as said below
- coloring: int32 [131072], P(('pts', 'grp')), may hold values 0 or 1
- damping: float32 [1], replicated, may hold values from 0.5 to 4
Outputs:
- cam_step: float32 [6, 131072], P(None, ('pts', 'grp'))
- point_step: float32 [3, 524288], P(None, ('pts', 'grp'))
Inputs may be any that keep to these rules, and one draw needn't show every extreme that they name: `requests`: in each row of a device toward one owner the live entries come first and name distinct cameras; any device may fill all 4 slots toward any owner device, and every device fills all 4 slots toward one owner device common to all devices. `obs_slot`: every entry names a live slot of its device's request table; the 4 observations of a point name distinct slots.
All inputs are finite; a program needn't handle non-finite values. No bound on the sum of `coloring` on one device may be relied on, other than what follows from the above.
Results may differ from a plain program's by a relative error of at most 0.0003.
Values sent between devices are 32-bit elements; how exact they have to be, the bound alone decides.
No kernel may reach another device: no remote copies, remote signals or barrier semaphores. Data moves between devices by JAX's collectives and lax.ppermute only.
A program may use at most 64 MiB of HBM per device.

v0:
```python
import jax
import jax.numpy as jnp
from jax import lax
from jax.sharding import PartitionSpec as P

ROUNDS = 2


UPPER = [(first, second) for first in range(6) for second in range(first, 6)]


def pack_sym(matrix):
    return jnp.stack([matrix[first, second] for first, second in UPPER])


def unpack_sym(packed):
    rows = []
    for first in range(6):
        rows.append(
            jnp.stack(
                [
                    packed[UPPER.index((min(first, second), max(first, second)))]
                    for second in range(6)
                ]
            )
        )
    return jnp.stack(rows)


def invert_three(matrix):
    c00 = matrix[1, 1] * matrix[2, 2] - matrix[1, 2] * matrix[2, 1]
    c01 = matrix[1, 2] * matrix[2, 0] - matrix[1, 0] * matrix[2, 2]
    c02 = matrix[1, 0] * matrix[2, 1] - matrix[1, 1] * matrix[2, 0]
    c11 = matrix[0, 0] * matrix[2, 2] - matrix[0, 2] * matrix[2, 0]
    c12 = matrix[0, 2] * matrix[1, 0] - matrix[0, 0] * matrix[1, 2]
    c22 = matrix[0, 0] * matrix[1, 1] - matrix[0, 1] * matrix[1, 0]
    determinant = matrix[0, 0] * c00 + matrix[0, 1] * c01 + matrix[0, 2] * c02
    rows = [[c00, c01, c02], [c01, c11, c12], [c02, c12, c22]]
    return jnp.stack([jnp.stack([entry / determinant for entry in line]) for line in rows])


def cholesky_six(matrix):
    lower = {}
    for first in range(6):
        for second in range(first + 1):
            total = matrix[first, second]
            for inner in range(second):
                total = total - lower[first, inner] * lower[second, inner]
            if first == second:
                lower[first, first] = jnp.sqrt(total)
            else:
                lower[first, second] = total / lower[second, second]
    return lower


def solve_six(lower, target):
    middle = []
    for first in range(6):
        total = target[first]
        for inner in range(first):
            total = total - lower[first, inner] * middle[inner]
        middle.append(total / lower[first, first])
    result = [None] * 6
    for first in reversed(range(6)):
        total = middle[first]
        for inner in range(first + 1, 6):
            total = total - lower[inner, first] * result[inner]
        result[first] = total / lower[first, first]
    return jnp.stack(result)


def point_geometry(jac_cam, jac_pt, resid, damp_value):
    camera_part = jac_cam.reshape((2, 6) + jac_cam.shape[1:])
    point_part = jac_pt.reshape((2, 3) + jac_pt.shape[1:])
    coupling = jnp.sum(camera_part[:, :, None] * point_part[:, None, :], axis=0)
    normal = jnp.sum(point_part[:, :, None] * point_part[:, None, :], axis=(0, 3))
    normal = normal + damp_value * jnp.eye(3, dtype=jac_pt.dtype)[:, :, None]
    point_inverse = invert_three(normal)
    point_rhs = -jnp.sum(point_part * resid[:, None], axis=(0, 2))
    return (camera_part, coupling, point_inverse, point_rhs)


def camera_terms(camera_part, coupling, point_inverse, point_rhs, resid):
    weighted = jnp.sum(coupling[:, :, None] * point_inverse[None, :, :, None, :], axis=1)
    schur_part = jnp.sum(weighted[:, None] * coupling[None], axis=2)
    camera_block = jnp.sum(camera_part[:, :, None] * camera_part[:, None, :], axis=0)
    camera_rhs = -jnp.sum(camera_part * resid[:, None], axis=0) - jnp.sum(
        weighted * point_rhs[None, :, None, :], axis=1
    )
    return jnp.concatenate([pack_sym(camera_block), pack_sym(schur_part), camera_rhs], axis=0)


def point_side(coupling, obs_steps):
    return jnp.sum(coupling * obs_steps[:, None], axis=(0, 2))


def camera_side(coupling, point_inverse, point_sum):
    solved = jnp.sum(point_inverse * point_sum[None], axis=1)
    return jnp.sum(coupling * solved[None, :, None, :], axis=1)


def owner_setup(totals, damp_value):
    upper_block = unpack_sym(totals[:21]) + damp_value * jnp.eye(6, dtype=totals.dtype)[:, :, None]
    diagonal_block = upper_block - unpack_sym(totals[21:42])
    return (upper_block, cholesky_six(diagonal_block), totals[42:48])


def owner_sum(received, owner_index, segments):
    features = received.shape[0]
    summed = jax.ops.segment_sum(
        received.reshape(features, -1).T, owner_index.reshape(-1), num_segments=segments + 1
    )
    return summed[:segments].T


def shards(jac_cam, jac_pt, resid, obs_slot, requests, coloring, damping):
    damp_value = damping[0]
    table = requests[0]
    cam_count = coloring.shape[0]
    slot_count = table.size
    flat_slots = obs_slot.reshape(-1)
    camera_part, coupling, point_inverse, point_rhs = point_geometry(
        jac_cam, jac_pt, resid, damp_value
    )
    terms = camera_terms(camera_part, coupling, point_inverse, point_rhs, resid)

    def slot_totals(values):
        features = values.shape[0]
        summed = jax.ops.segment_sum(
            values.reshape(features, -1).T, flat_slots, num_segments=slot_count
        ).T
        return summed.reshape((features,) + table.shape)

    def at_observations(slot_values):
        return jnp.take(slot_values.reshape(slot_values.shape[0], -1), obs_slot, axis=1)

    served = lax.all_to_all(
        lax.all_to_all(table, "pts", split_axis=2, concat_axis=2, tiled=True),
        "grp",
        split_axis=0,
        concat_axis=0,
        tiled=True,
    )
    valid = served >= 0
    owner_index = jnp.where(valid, served, cam_count)
    blocks_back = lax.all_to_all(
        lax.all_to_all(slot_totals(terms), "pts", split_axis=3, concat_axis=3, tiled=True),
        "grp",
        split_axis=1,
        concat_axis=1,
        tiled=True,
    )
    totals = owner_sum(blocks_back, owner_index, cam_count)

    def share_steps(step_values):
        reply = jnp.where(
            valid[None], jnp.take(step_values, jnp.where(valid, served, 0), axis=1), 0.0
        )
        arrived = lax.all_to_all(
            lax.all_to_all(reply, "pts", split_axis=3, concat_axis=3, tiled=True),
            "grp",
            split_axis=1,
            concat_axis=1,
            tiled=True,
        )
        return at_observations(arrived)

    upper_block, factor, camera_rhs = owner_setup(totals, damp_value)
    colors = [coloring == 0, coloring == 1]
    steps = jnp.where(colors[0][None], solve_six(factor, camera_rhs), 0.0)
    for sweep in range(2 * ROUNDS - 1):
        current = colors[(sweep + 1) % 2]
        point_sum = point_side(coupling, share_steps(steps))
        pushed = camera_side(coupling, point_inverse, point_sum)
        back = lax.all_to_all(
            lax.all_to_all(slot_totals(pushed), "pts", split_axis=3, concat_axis=3, tiled=True),
            "grp",
            split_axis=1,
            concat_axis=1,
            tiled=True,
        )
        product = jnp.sum(upper_block * steps[None], axis=1) - owner_sum(
            back, owner_index, cam_count
        )
        steps = steps + jnp.where(current[None], solve_six(factor, camera_rhs - product), 0.0)
    point_sum = point_side(coupling, share_steps(steps))
    point_step = jnp.sum(point_inverse * (point_rhs - point_sum)[None], axis=1)
    return (steps, point_step)


def solution(mesh):
    return jax.shard_map(
        shards,
        mesh=mesh,
        in_specs=(
            P(None, None, ("pts", "grp")),
            P(None, None, ("pts", "grp")),
            P(None, None, ("pts", "grp")),
            P(None, ("pts", "grp")),
            P("grp", None, None, "pts"),
            P(("pts", "grp")),
            P(),
        ),
        out_specs=(P(None, ("pts", "grp")), P(None, ("pts", "grp"))),
        check_vma=False,
    )
```

profile of v0, /device:TPU:1, one launch (start us, length us, event | category | flops | bytes accessed | tf_op | source)
XLA Modules:
  0.0 860.8 jit_solution(12149952349665627181)
XLA Ops:
  2.2 20.4 %all-to-all-start = ((s32[4,4,128]{1,0,2:T(4,128)}), s32[4,4,128]{1,0,2:T(4,128)S(1)}, u32[]{:S(2)}, u32[]{:S(2)}) async-start(s32[4,4,128]{1,0,2:T(4,128)} %bitcast), calls=%async_computation | async-start | bytes 524288 | tf_op jit(solution)/shard_map/all_to_all | solution.py:138
  30.3 12.7 %all-to-all-done = s32[4,4,128]{1,0,2:T(4,128)S(1)} async-done(((s32[4,4,128]{1,0,2:T(4,128)}), s32[4,4,128]{1,0,2:T(4,128)S(1)}, u32[]{:S(2)}, u32[]{:S(2)}) %all-to-all-start) | async-done | bytes 8224 | tf_op jit(solution)/shard_map/all_to_all | solution.py:138
  50.6 22.6 %scatter_custom_fusion = f32[2048,48]{1,0:T(8,128)S(1)} fusion(s32[4096]{0:T(1024)S(1)} %bitcast.713, f32[4096,48]{1,0:T(8,128)S(1)} %copy.672, f32[]{:T(128)} %constant.7.clone.1), kind=kCustom, calls=%fused_computation.38 | custom fusion | flops 196608 | bytes 393220 | tf_op jit(solution)/shard_map/scatter-add | solution.py:129
  75.8 8.6 all-to-all-start.2
  85.1 24.7 %all-to-all-done.2 = f32[128,1,768]{2,1,0:T(1,128)S(1)} async-done(((f32[128,1,768]{2,1,0:T(1,128)}), f32[128,1,768]{2,1,0:T(1,128)S(1)}, u32[]{:S(2)}, u32[]{:S(2)}) %all-to-all-start.2) | async-done | bytes 393248 | tf_op jit(solution)/shard_map/all_to_all | solution.py:147
  126.0 11.5 %scatter_custom_fusion.1 = f32[257,48]{1,0:T(8,128)S(1)} fusion(s32[2048]{0:T(1024)S(1)} %bitcast.717, f32[2048,48]{1,0:T(8,128)S(1)} %copy.676, f32[]{:T(128)} %constant.7.clone.1), kind=kCustom, calls=%fused_computation.59 | custom fusion | flops 98304 | bytes 49348 | tf_op jit(solution)/shard_map/scatter-add | solution.py:110
  148.8 10.8 %all-to-all-start.4 = ((f32[6,4,4,128]{0,2,1,3:T(4,128)}), f32[6,4,4,128]{0,2,1,3:T(4,128)S(1)}, u32[]{:S(2)}, u32[]{:S(2)}) async-start(f32[6,4,4,128]{0,2,1,3:T(4,128)} %bitcast_select_fusion.3), calls=%async_computation.4 | async-start | bytes 2097152 | tf_op jit(solution)/shard_map/all_to_all | solution.py:160
  159.6 52.1 %all-to-all-done.4 = f32[6,4,4,128]{0,2,1,3:T(4,128)S(1)} async-done(((f32[6,4,4,128]{0,2,1,3:T(4,128)}), f32[6,4,4,128]{0,2,1,3:T(4,128)S(1)}, u32[]{:S(2)}, u32[]{:S(2)}) %all-to-all-start.4) | async-done | bytes 49184 | tf_op jit(solution)/shard_map/all_to_all | solution.py:160
  221.2 14.2 %gather_fusion.1 = f32[4096,6]{1,0:T(8,128)} fusion(f32[6,2048]{0,1:T(8,128)S(1)} %bitcast.632, s32[4096]{0:T(1024)S(1)} %bitcast_clamp_fusion), kind=kCustom, calls=%fused_computation.1.clone | custom fusion | bytes 212992 | tf_op jit(solution)/shard_map/jit(_take)/gather | solution.py:135
  239.8 22.7 %scatter_custom_fusion.2 = f32[2048,6]{1,0:T(8,128)S(1)} fusion(s32[4096]{0:T(1024)} %bitcast.714, f32[4096,6]{1,0:T(8,128)S(1)} %bitcast.644, f32[]{:T(128)} %constant.7.clone.1), kind=kCustom, calls=%fused_computation.36 | custom fusion | flops 24576 | bytes 49664 | tf_op jit(solution)/shard_map/scatter-add | solution.py:129
  263.2 63.0 %all_to_all.90 = f32[6,4,4,128]{0,2,1,3:T(4,128)S(1)} all-to-all(f32[6,4,4,128]{0,2,1,3:T(4,128)S(1)} %copy.687), channel_id=1, replica_groups=mesh['pts'=128,'grp'=4] {'pts'}, dimensions={3} | all-to-all | bytes 98304 | tf_op jit(solution)/shard_map/all_to_all | solution.py:176
  335.7 11.6 %scatter_custom_fusion.3 = f32[257,6]{1,0:T(8,128)S(1)} fusion(s32[2048]{0:T(1024)} %bitcast.718, f32[2048,6]{1,0:T(8,128)S(1)} %copy.690, f32[]{:T(128)} %constant.7.clone.1), kind=kCustom, calls=%fused_computation.57 | custom fusion | flops 12288 | bytes 6680 | tf_op jit(solution)/shard_map/scatter-add | solution.py:110
  357.4 63.2 %all_to_all.91 = f32[6,4,4,128]{0,2,1,3:T(4,128)S(1)} all-to-all(f32[6,4,4,128]{0,2,1,3:T(4,128)S(1)} %bitcast_select_fusion.2), channel_id=1, replica_groups=mesh['pts'=128,'grp'=4] {'pts'}, dimensions={3} | all-to-all | bytes 98304 | tf_op jit(solution)/shard_map/all_to_all | solution.py:160
  428.2 14.2 %gather_fusion.3 = f32[4096,6]{1,0:T(8,128)} fusion(f32[6,2048]{0,1:T(8,128)S(1)} %bitcast.633, s32[4096]{0:T(1024)S(1)} %copy-done.22), kind=kCustom, calls=%fused_computation.5.clone | custom fusion | bytes 212992 | tf_op jit(solution)/shard_map/jit(_take)/gather | solution.py:135
  446.7 22.7 %scatter_custom_fusion.4 = f32[2048,6]{1,0:T(8,128)S(1)} fusion(s32[4096]{0:T(1024)} %bitcast.715, f32[4096,6]{1,0:T(8,128)S(1)} %bitcast.645, f32[]{:T(128)} %constant.7.clone.1), kind=kCustom, calls=%fused_computation.34 | custom fusion | flops 24576 | bytes 49664 | tf_op jit(solution)/shard_map/scatter-add | solution.py:129
  470.2 63.0 %all_to_all.93 = f32[6,4,4,128]{0,2,1,3:T(4,128)S(1)} all-to-all(f32[6,4,4,128]{0,2,1,3:T(4,128)S(1)} %copy.700), channel_id=1, replica_groups=mesh['pts'=128,'grp'=4] {'pts'}, dimensions={3} | all-to-all | bytes 98304 | tf_op jit(solution)/shard_map/all_to_all | solution.py:176
  542.6 11.6 %scatter_custom_fusion.5 = f32[257,6]{1,0:T(8,128)S(1)} fusion(s32[2048]{0:T(1024)} %bitcast.719, f32[2048,6]{1,0:T(8,128)S(1)} %copy.703, f32[]{:T(128)} %constant.7.clone.1), kind=kCustom, calls=%fused_computation.55 | custom fusion | flops 12288 | bytes 6680 | tf_op jit(solution)/shard_map/scatter-add | solution.py:110
  564.3 63.0 %all_to_all.94 = f32[6,4,4,128]{0,2,1,3:T(4,128)S(1)} all-to-all(f32[6,4,4,128]{0,2,1,3:T(4,128)S(1)} %bitcast_select_fusion.1), channel_id=1, replica_groups=mesh['pts'=128,'grp'=4] {'pts'}, dimensions={3} | all-to-all | bytes 98304 | tf_op jit(solution)/shard_map/all_to_all | solution.py:160
  635.0 14.2 %gather_fusion.5 = f32[4096,6]{1,0:T(8,128)} fusion(f32[6,2048]{0,1:T(8,128)S(1)} %bitcast.634, s32[4096]{0:T(1024)S(1)} %copy-done.23), kind=kCustom, calls=%fused_computation.6.clone | custom fusion | bytes 212992 | tf_op jit(solution)/shard_map/jit(_take)/gather | solution.py:135
  653.5 22.7 %scatter_custom_fusion.6 = f32[2048,6]{1,0:T(8,128)S(1)} fusion(s32[4096]{0:T(1024)} %bitcast.716, f32[4096,6]{1,0:T(8,128)S(1)} %bitcast.643, f32[]{:T(128)} %constant.7.clone.1), kind=kCustom, calls=%fused_computation.32 | custom fusion | flops 24576 | bytes 49664 | tf_op jit(solution)/shard_map/scatter-add | solution.py:129
  676.9 63.0 %all_to_all.96 = f32[6,4,4,128]{0,2,1,3:T(4,128)S(1)} all-to-all(f32[6,4,4,128]{0,2,1,3:T(4,128)S(1)} %copy.713), channel_id=1, replica_groups=mesh['pts'=128,'grp'=4] {'pts'}, dimensions={3} | all-to-all | bytes 98304 | tf_op jit(solution)/shard_map/all_to_all | solution.py:176
  749.4 11.6 %scatter_custom_fusion.7 = f32[257,6]{1,0:T(8,128)S(1)} fusion(s32[2048]{0:T(1024)} %bitcast.720, f32[2048,6]{1,0:T(8,128)S(1)} %copy.716, f32[]{:T(128)} %constant.7.clone.1), kind=kCustom, calls=%fused_computation.53 | custom fusion | flops 12288 | bytes 6680 | tf_op jit(solution)/shard_map/scatter-add | solution.py:110
  771.0 63.3 %all_to_all.97 = f32[6,4,4,128]{0,2,1,3:T(4,128)S(1)} all-to-all(f32[6,4,4,128]{0,2,1,3:T(4,128)S(1)} %bitcast_select_fusion), channel_id=1, replica_groups=mesh['pts'=128,'grp'=4] {'pts'}, dimensions={3} | all-to-all | bytes 98304 | tf_op jit(solution)/shard_map/all_to_all | solution.py:160
  842.0 14.2 %gather_fusion.7 = f32[4096,6]{1,0:T(8,128)} fusion(f32[6,2048]{0,1:T(8,128)S(1)} %bitcast.631, s32[4096]{0:T(1024)S(1)} %copy-done.24), kind=kCustom, calls=%fused_computation.7.clone | custom fusion | bytes 212992 | tf_op jit(solution)/shard_map/jit(_take)/gather | solution.py:135
  (474 shorter events, 154.6 us)
Async XLA Ops:
  2.2 40.8 %all-to-all-start = ((s32[4,4,128]{1,0,2:T(4,128)}), s32[4,4,128]{1,0,2:T(4,128)S(1)}, u32[]{:S(2)}, u32[]{:S(2)}) async-start(s32[4,4,128]{1,0,2:T(4,128)} %bitcast), calls=%async_computation | async-start | bytes 524288 | tf_op jit(solution)/shard_map/all_to_all | solution.py:138
  43.8 32.1 %all-to-all-start.1 = ((s32[4,4,128]{2,1,0:T(4,128)}), s32[4,4,128]{2,1,0:T(4,128)S(1)}, u32[]{:S(2)}, u32[]{:S(2)}) async-start(s32[4,4,128]{2,1,0:T(4,128)} %copy.671), calls=%async_computation.1 | async-start | bytes 16384 | tf_op jit(solution)/shard_map/all_to_all | solution.py:137
  75.8 34.0 %all-to-all-start.2 = ((f32[128,1,768]{2,1,0:T(1,128)}), f32[128,1,768]{2,1,0:T(1,128)S(1)}, u32[]{:S(2)}, u32[]{:S(2)}) async-start(f32[128,1,768]{2,1,0:T(1,128)} %reshape.2628), calls=%async_computation.2 | async-start | bytes 786432 | tf_op jit(solution)/shard_map/all_to_all | solution.py:147
  84.4 53.5 %copy-start.42 = (f32[6,6]{1,0:T(8,128)}, f32[6,6]{1,0:T(8,128)S(1)}, u32[]{:S(2)}) copy-start(f32[6,6]{1,0:T(8,128)S(1)} %fusion.21) | copy-start | bytes 436
  85.0 54.1 %copy-start.123 = (pred[256]{0:T(512)(128)(4,1)}, pred[256]{0:T(512)(128)(4,1)S(1)}, u32[]{:S(2)}) copy-start(pred[256]{0:T(512)(128)(4,1)S(1)} %get-tuple-element.197) | copy-start | bytes 772
  85.1 41.0 %copy-start.122 = (s32[4,4,128]{2,1,0:T(4,128)}, s32[4,4,128]{2,1,0:T(4,128)S(1)}, u32[]{:S(2)}) copy-start(s32[4,4,128]{2,1,0:T(4,128)S(1)} %get-tuple-element.190) | copy-start | bytes 24580
  114.4 11.0 %all-to-all-start.3 = ((f32[48,4,4,128]{3,0,2,1:T(8,128)}), f32[48,4,4,128]{3,0,2,1:T(8,128)S(1)}, u32[]{:S(2)}, u32[]{:S(2)}) async-start(f32[48,4,4,128]{3,0,2,1:T(8,128)} %copy.674), calls=%async_computation.3 | async-start | bytes 786432 | tf_op jit(solution)/shard_map/all_to_all | solution.py:146
  148.8 67.7 %copy-start.33 = (s32[4,1024]{1,0:T(4,128)S(1)}, s32[4,1024]{1,0:T(4,128)}, u32[]{:S(2)}) copy-start(s32[4,1024]{1,0:T(4,128)} %param.14) | copy-start | bytes 49156
  148.8 62.9 %all-to-all-start.4 = ((f32[6,4,4,128]{0,2,1,3:T(4,128)}), f32[6,4,4,128]{0,2,1,3:T(4,128)S(1)}, u32[]{:S(2)}, u32[]{:S(2)}) async-start(f32[6,4,4,128]{0,2,1,3:T(4,128)} %bitcast_select_fusion.3), calls=%async_computation.4 | async-start | bytes 2097152 | tf_op jit(solution)/shard_map/all_to_all | solution.py:160
  159.6 75.8 %copy-start.21 = (s32[4096]{0:T(1024)}, s32[4096]{0:T(1024)S(1)}, u32[]{:S(2)}) copy-start(s32[4096]{0:T(1024)S(1)} %bitcast_clamp_fusion) | copy-start | bytes 49156
  212.9 8.0 all-to-all-start.5
  263.2 67.7 %copy-start.43 = (f32[6,6]{1,0:T(8,128)S(1)}, f32[6,6]{1,0:T(8,128)}, u32[]{:S(2)}) copy-start(f32[6,6]{1,0:T(8,128)} %copy-done.42) | copy-start | bytes 436
  263.2 67.7 %copy-start.47 = (f32[6,256]{1,0:T(8,128)S(1)}, f32[6,256]{1,0:T(8,128)}, u32[]{:S(2)}) copy-start(f32[6,256]{1,0:T(8,128)} %copy-done.46) | copy-start | bytes 18436
  327.6 7.6 all-to-all-start.7
  357.4 70.9 %copy-start.22 = (s32[4096]{0:T(1024)S(1)}, s32[4096]{0:T(1024)}, u32[]{:S(2)}) copy-start(s32[4096]{0:T(1024)} %copy-done.21) | copy-start | bytes 49156
  470.2 67.7 %copy-start.37 = (f32[6,256]{1,0:T(8,128)S(1)}, f32[6,256]{1,0:T(8,128)}, u32[]{:S(2)}) copy-start(f32[6,256]{1,0:T(8,128)} %copy-done.36) | copy-start | bytes 18436
  470.2 67.7 %copy-start.44 = (f32[6,6]{1,0:T(8,128)S(1)}, f32[6,6]{1,0:T(8,128)}, u32[]{:S(2)}) copy-start(f32[6,6]{1,0:T(8,128)} %copy-done.42) | copy-start | bytes 436
  534.6 7.6 all-to-all-start.11
  564.3 70.7 %copy-start.23 = (s32[4096]{0:T(1024)S(1)}, s32[4096]{0:T(1024)}, u32[]{:S(2)}) copy-start(s32[4096]{0:T(1024)} %copy-done.21) | copy-start | bytes 49156
  676.9 67.7 %copy-start.35 = (f32[6,256]{1,0:T(8,128)S(1)}, f32[6,256]{1,0:T(8,128)}, u32[]{:S(2)}) copy-start(f32[6,256]{1,0:T(8,128)} %copy-done.34) | copy-start | bytes 18436
  676.9 67.7 %copy-start.45 = (f32[6,6]{1,0:T(8,128)S(1)}, f32[6,6]{1,0:T(8,128)}, u32[]{:S(2)}) copy-start(f32[6,6]{1,0:T(8,128)} %copy-done.42) | copy-start | bytes 436
  741.3 7.6 all-to-all-start.15
  763.5 70.8 %copy-start.102 = (f32[6,256]{1,0:T(8,128)}, f32[6,256]{1,0:T(8,128)S(1)}, u32[]{:S(2)}) copy-start(f32[6,256]{1,0:T(8,128)S(1)} %select_add_fusion) | copy-start | bytes 18436
  771.0 70.9 %copy-start.24 = (s32[4096]{0:T(1024)S(1)}, s32[4096]{0:T(1024)}, u32[]{:S(2)}) copy-start(s32[4096]{0:T(1024)} %copy-done.21) | copy-start | bytes 49156
  (114 other events, 1745.8 us)
where the time goes:
time: 875 us; the launch traced here: 861 us
  blocking collectives  399 us (46%)
  other arithmetic  174 us (20%)
  waiting for transfers between devices  113 us (13%)
  local copies, waits for them, and re-layouts  109 us (12%)
  starting transfers between devices  62 us (7%)
    all_to_all x3, blocking collectives, share_steps(): lax.all_to_all(reply, 'pts', split_axis=3, concat_axis=3, tiled=True)  189 us
    all_to_all x3, blocking collectives, shards(): lax.all_to_all(slot_totals(pushed), 'pts', split_axis=3, concat_axis=3, t...  189 us
    scatter-add x4, other arithmetic, slot_totals(): jax.ops.segment_sum(values.reshape(features, -1).T, flat_slots, num_segme...  90.8 us
    gather x4, local copies, waits for them, and re-layouts, at_observations(): jnp.take(slot_values.reshape(slot_values.shape[0], -1), obs_slot, axis=1)  56.7 us
    all_to_all x1, waiting for transfers between devices, share_steps(): lax.all_to_all(reply, 'pts', split_axis=3, concat_axis=3, tiled=True)  52.1 us
    scatter-add x4, other arithmetic, owner_sum(): jax.ops.segment_sum(received.reshape(features, -1).T, owner_index.reshape...  46.3 us
    all_to_all x1, waiting for transfers between devices, shards(): lax.all_to_all(slot_totals(terms), 'pts', split_axis=3, concat_axis=3, ti...  24.7 us
    gather x4, local copies, waits for them, and re-layouts, share_steps(): jnp.take(step_values, jnp.where(valid, served, 0), axis=1)  21.9 us
  transfers between devices with their start and end apart: 9, of which 8 were waited for; matrix products, arithmetic and copies ran while one was open for 4% of the time, Pallas kernels for 0%

commit v1 on v0

--- a/solution.py
+++ b/solution.py
@@ -1,7 +1,7 @@
 import jax
 import jax.numpy as jnp
 from jax import lax
-from jax.sharding import PartitionSpec as P
+from jax.sharding import Mesh, PartitionSpec as P
 
 ROUNDS = 2
 
@@ -113,6 +113,17 @@
     return summed[:segments].T
 
 
+def exchange(values):
+    features, groups, places, lanes = values.shape
+    inner = lanes // OUTER
+    t = values.reshape(features, groups, places, OUTER, inner).transpose(4, 1, 3, 2, 0)
+    t = t.reshape(inner * groups, OUTER, places, features)
+    t = lax.all_to_all(t, INNER_AXES, 0, 0, tiled=True)
+    t = lax.all_to_all(t, "z", 1, 1, tiled=True)
+    t = t.reshape(inner, groups, OUTER, places, features).transpose(4, 1, 3, 2, 0)
+    return t.reshape(features, groups, places, lanes)
+
+
 def shards(jac_cam, jac_pt, resid, obs_slot, requests, coloring, damping):
     damp_value = damping[0]
     table = requests[0]
@@ -134,35 +145,19 @@
     def at_observations(slot_values):
         return jnp.take(slot_values.reshape(slot_values.shape[0], -1), obs_slot, axis=1)
 
-    served = lax.all_to_all(
-        lax.all_to_all(table, "pts", split_axis=2, concat_axis=2, tiled=True),
-        "grp",
-        split_axis=0,
-        concat_axis=0,
-        tiled=True,
-    )
+    sent = jnp.concatenate([slot_totals(terms), table[None].astype(terms.dtype)], axis=0)
+    arrived_all = exchange(sent)
+    blocks_back = arrived_all[:-1]
+    served = arrived_all[-1].astype(jnp.int32)
     valid = served >= 0
     owner_index = jnp.where(valid, served, cam_count)
-    blocks_back = lax.all_to_all(
-        lax.all_to_all(slot_totals(terms), "pts", split_axis=3, concat_axis=3, tiled=True),
-        "grp",
-        split_axis=1,
-        concat_axis=1,
-        tiled=True,
-    )
     totals = owner_sum(blocks_back, owner_index, cam_count)
 
     def share_steps(step_values):
         reply = jnp.where(
             valid[None], jnp.take(step_values, jnp.where(valid, served, 0), axis=1), 0.0
         )
-        arrived = lax.all_to_all(
-            lax.all_to_all(reply, "pts", split_axis=3, concat_axis=3, tiled=True),
-            "grp",
-            split_axis=1,
-            concat_axis=1,
-            tiled=True,
-        )
+        arrived = exchange(reply)
         return at_observations(arrived)
 
     upper_block, factor, camera_rhs = owner_setup(totals, damp_value)
@@ -172,13 +167,7 @@
         current = colors[(sweep + 1) % 2]
         point_sum = point_side(coupling, share_steps(steps))
         pushed = camera_side(coupling, point_inverse, point_sum)
-        back = lax.all_to_all(
-            lax.all_to_all(slot_totals(pushed), "pts", split_axis=3, concat_axis=3, tiled=True),
-            "grp",
-            split_axis=1,
-            concat_axis=1,
-            tiled=True,
-        )
+        back = exchange(slot_totals(pushed))
         product = jnp.sum(upper_block * steps[None], axis=1) - owner_sum(
             back, owner_index, cam_count
         )
@@ -188,19 +177,26 @@
     return (steps, point_step)
 
 
+OUTER = 16
+INNER_AXES = ("x", "c", "y")
+
+
 def solution(mesh):
+    npts, ngrp = mesh.shape["pts"], mesh.shape["grp"]
+    split = Mesh(mesh.devices.reshape(OUTER, npts // OUTER, 1, ngrp), ("z", "x", "c", "y"))
+    every = ("z", "x", "c", "y")
     return jax.shard_map(
         shards,
-        mesh=mesh,
+        mesh=split,
         in_specs=(
-            P(None, None, ("pts", "grp")),
-            P(None, None, ("pts", "grp")),
-            P(None, None, ("pts", "grp")),
-            P(None, ("pts", "grp")),
-            P("grp", None, None, "pts"),
-            P(("pts", "grp")),
+            P(None, None, every),
+            P(None, None, every),
+            P(None, None, every),
+            P(None, every),
+            P("y", None, None, ("z", "x", "c")),
+            P(every),
             P(),
         ),
-        out_specs=(P(None, ("pts", "grp")), P(None, ("pts", "grp"))),
+        out_specs=(P(None, every), P(None, every)),
         check_vma=False,
     )

time: 875 us -> 578 us (0.66)
  blocking collectives: 399 us -> 134 us
  waiting for transfers between devices: 113 us -> 69.5 us
  local copies, waits for them, and re-layouts: 109 us -> 139 us
  starting transfers between devices: 62 us -> 40.4 us
    all_to_all x9 -> x10, blocking collectives: 399 us -> 134 us  [the longest x7 91.9 us: exchange(): t = lax.all_to_all(t, INNER_AXES, 0, 0, tiled=True)]
    all_to_all x9 -> x6, waiting for transfers between devices: 113 us -> 69.5 us  [the longest x5 62.3 us: exchange(): t = lax.all_to_all(t, 'z', 1, 1, tiled=True)]
    all_to_all x9 -> x6, starting transfers between devices: 62 us -> 40.4 us  [the longest x5 29.9 us: exchange(): t = lax.all_to_all(t, 'z', 1, 1, tiled=True)]
    unnamed x316 -> x319, local copies, waits for them, and re-layouts: 8.48 us -> 21.1 us
    all_to_all x1 -> x16, other arithmetic: 1.57 us -> 13.4 us  [the longest x8 6.72 us: exchange(): t = lax.all_to_all(t, INNER_AXES, 0, 0, tiled=True)]
    gather x4 -> x8, local copies, waits for them, and re-layouts: 21.9 us -> 23.2 us  [share_steps(): jnp.take(step_values, jnp.where(valid, served, 0), axis=1)]
  transfers between devices with their start and end apart: 9 -> 6, of which waited for: 8 -> 6; matrix products, arithmetic and copies ran while one was open for 4% -> 0% of each run, Pallas kernels for 0% -> 0%
where the time goes in v1:
time: 578 us; the launch traced here: 569 us
  other arithmetic  180 us (31%)
  local copies, waits for them, and re-layouts  139 us (24%)
  blocking collectives  134 us (23%)
  waiting for transfers between devices  69.5 us (12%)
  starting transfers between devices  40.4 us (7%)
    all_to_all x7, blocking collectives, exchange(): t = lax.all_to_all(t, INNER_AXES, 0, 0, tiled=True)  91.9 us
    scatter-add x4, other arithmetic, slot_totals(): jax.ops.segment_sum(values.reshape(features, -1).T, flat_slots, num_segme...  91.3 us
    all_to_all x5, waiting for transfers between devices, exchange(): t = lax.all_to_all(t, 'z', 1, 1, tiled=True)  62.3 us
    gather x4, local copies, waits for them, and re-layouts, at_observations(): jnp.take(slot_values.reshape(slot_values.shape[0], -1), obs_slot, axis=1)  56.3 us
    scatter-add x4, other arithmetic, owner_sum(): jax.ops.segment_sum(received.reshape(features, -1).T, owner_index.reshape...  46.7 us
    all_to_all x3, blocking collectives, exchange(): t = lax.all_to_all(t, 'z', 1, 1, tiled=True)  42.3 us
    all_to_all x5, starting transfers between devices, exchange(): t = lax.all_to_all(t, 'z', 1, 1, tiled=True)  29.9 us
    gather x8, local copies, waits for them, and re-layouts, share_steps(): jnp.take(step_values, jnp.where(valid, served, 0), axis=1)  23.2 us
  transfers between devices with their start and end apart: 6, of which 6 were waited for; matrix products, arithmetic and copies ran while one was open for 0% of the time, Pallas kernels for 0%

profile of v1, /device:TPU:1, one launch (start us, length us, event | category | flops | bytes accessed | tf_op | source)
XLA Modules:
  0.0 568.8 jit_solution(11985948154704169987)
XLA Ops:
  13.7 22.9 %scatter_custom_fusion = f32[2048,48]{1,0:T(8,128)S(1)} fusion(s32[4096]{0:T(1024)S(1)} %bitcast.861, f32[4096,48]{1,0:T(8,128)} %copy.826, f32[]{:T(128)} %constant.7.clone.1), kind=kCustom, calls=%fused_computation.31 | custom fusion | flops 196608 | bytes 393728 | tf_op jit(solution)/shard_map/scatter-add | solution.py:140
  38.5 20.0 %all_to_all.80 = f32[32,1,3136]{2,1,0:T(1,128)S(1)} all-to-all(f32[32,1,3136]{2,1,0:T(1,128)S(1)} %reshape.2693), channel_id=1, replica_groups=mesh['z'=16,'x'=8,'c'=1,'y'=4] {'x','c','y'}, dimensions={0} | all-to-all | bytes 802816 | tf_op jit(solution)/shard_map/all_to_all | solution.py:121
  64.8 13.7 %all-to-all-start.1 = ((f32[16,1,6272]{2,1,0:T(1,128)}), f32[16,1,6272]{2,1,0:T(1,128)S(1)}, u32[]{:S(2)}, u32[]{:S(2)}) async-start(f32[16,1,6272]{2,1,0:T(1,128)} %reshape.2695), calls=%async_computation.1 | async-start | bytes 802816 | tf_op jit(solution)/shard_map/all_to_all | solution.py:122
  80.2 16.6 %all-to-all-done.1 = f32[16,1,6272]{2,1,0:T(1,128)S(1)} async-done(((f32[16,1,6272]{2,1,0:T(1,128)}), f32[16,1,6272]{2,1,0:T(1,128)S(1)}, u32[]{:S(2)}, u32[]{:S(2)}) %all-to-all-start.1) | async-done | bytes 401440 | tf_op jit(solution)/shard_map/all_to_all | solution.py:122
  112.0 11.9 %scatter_custom_fusion.1 = f32[257,48]{1,0:T(8,128)S(1)} fusion(s32[2048]{0:T(1024)S(1)} %bitcast.865, f32[2048,48]{1,0:T(8,128)S(1)} %bitcast.786, f32[]{:T(128)} %constant.7.clone.1), kind=kCustom, calls=%fused_computation.52 | custom fusion | flops 98304 | bytes 49348 | tf_op jit(solution)/shard_map/scatter-add | solution.py:110
  173.0 14.1 %gather_fusion.1 = f32[4096,6]{1,0:T(8,128)} fusion(f32[6,2048]{0,1:T(8,128)S(1)} %bitcast.734, s32[4096]{0:T(1024)S(1)} %bitcast_clamp_fusion), kind=kCustom, calls=%fused_computation.1.clone | custom fusion | bytes 212992 | tf_op jit(solution)/shard_map/jit(_take)/gather | solution.py:146
  191.3 22.7 %scatter_custom_fusion.2 = f32[2048,6]{1,0:T(8,128)S(1)} fusion(s32[4096]{0:T(1024)} %bitcast.862, f32[4096,6]{1,0:T(8,128)S(1)} %bitcast.750, f32[]{:T(128)} %constant.7.clone.1), kind=kCustom, calls=%fused_computation.29 | custom fusion | flops 24576 | bytes 49664 | tf_op jit(solution)/shard_map/scatter-add | solution.py:140
  215.8 12.2 %all_to_all.81 = f32[32,1,384]{2,1,0:T(1,128)S(1)} all-to-all(f32[32,1,384]{2,1,0:T(1,128)S(1)} %reshape.2701), channel_id=1, replica_groups=mesh['z'=16,'x'=8,'c'=1,'y'=4] {'x','c','y'}, dimensions={0} | all-to-all | bytes 98304 | tf_op jit(solution)/shard_map/all_to_all | solution.py:121
  247.6 11.6 %scatter_custom_fusion.3 = f32[257,6]{1,0:T(8,128)S(1)} fusion(s32[2048]{0:T(1024)} %bitcast.866, f32[2048,6]{1,0:T(8,128)S(1)} %copy.851, f32[]{:T(128)} %constant.7.clone.1), kind=kCustom, calls=%fused_computation.50 | custom fusion | flops 12288 | bytes 6680 | tf_op jit(solution)/shard_map/scatter-add | solution.py:110
  269.8 11.8 %all_to_all.82 = f32[32,1,384]{2,1,0:T(1,128)S(1)} all-to-all(f32[32,1,384]{2,1,0:T(1,128)S(1)} %reshape.2705), channel_id=1, replica_groups=mesh['z'=16,'x'=8,'c'=1,'y'=4] {'x','c','y'}, dimensions={0} | all-to-all | bytes 98304 | tf_op jit(solution)/shard_map/all_to_all | solution.py:121
  283.0 14.1 %all_to_all.83 = f32[16,1,768]{2,1,0:T(1,128)S(1)} all-to-all(f32[16,1,768]{2,1,0:T(1,128)S(1)} %reshape.2707), channel_id=1, replica_groups=mesh['z'=16,'x'=8,'c'=1,'y'=4] {'z'}, dimensions={0} | all-to-all | bytes 98304 | tf_op jit(solution)/shard_map/all_to_all | solution.py:122
  299.0 14.1 %gather_fusion.3 = f32[4096,6]{1,0:T(8,128)} fusion(f32[6,2048]{0,1:T(8,128)S(1)} %bitcast.735, s32[4096]{0:T(1024)S(1)} %bitcast_clamp_fusion), kind=kCustom, calls=%fused_computation.5.clone | custom fusion | bytes 212992 | tf_op jit(solution)/shard_map/jit(_take)/gather | solution.py:146
  317.4 22.7 %scatter_custom_fusion.4 = f32[2048,6]{1,0:T(8,128)S(1)} fusion(s32[4096]{0:T(1024)} %bitcast.863, f32[4096,6]{1,0:T(8,128)S(1)} %bitcast.751, f32[]{:T(128)} %constant.7.clone.1), kind=kCustom, calls=%fused_computation.27 | custom fusion | flops 24576 | bytes 49664 | tf_op jit(solution)/shard_map/scatter-add | solution.py:140
  341.8 12.0 %all_to_all.84 = f32[32,1,384]{2,1,0:T(1,128)S(1)} all-to-all(f32[32,1,384]{2,1,0:T(1,128)S(1)} %reshape.2709), channel_id=1, replica_groups=mesh['z'=16,'x'=8,'c'=1,'y'=4] {'x','c','y'}, dimensions={0} | all-to-all | bytes 98304 | tf_op jit(solution)/shard_map/all_to_all | solution.py:121
  373.3 11.6 %scatter_custom_fusion.5 = f32[257,6]{1,0:T(8,128)S(1)} fusion(s32[2048]{0:T(1024)} %bitcast.867, f32[2048,6]{1,0:T(8,128)S(1)} %copy.868, f32[]{:T(128)} %constant.7.clone.1), kind=kCustom, calls=%fused_computation.48 | custom fusion | flops 12288 | bytes 6680 | tf_op jit(solution)/shard_map/scatter-add | solution.py:110
  395.4 11.9 %all_to_all.85 = f32[32,1,384]{2,1,0:T(1,128)S(1)} all-to-all(f32[32,1,384]{2,1,0:T(1,128)S(1)} %reshape.2713), channel_id=1, replica_groups=mesh['z'=16,'x'=8,'c'=1,'y'=4] {'x','c','y'}, dimensions={0} | all-to-all | bytes 98304 | tf_op jit(solution)/shard_map/all_to_all | solution.py:121
  408.7 14.1 %all_to_all.86 = f32[16,1,768]{2,1,0:T(1,128)S(1)} all-to-all(f32[16,1,768]{2,1,0:T(1,128)S(1)} %reshape.2715), channel_id=1, replica_groups=mesh['z'=16,'x'=8,'c'=1,'y'=4] {'z'}, dimensions={0} | all-to-all | bytes 98304 | tf_op jit(solution)/shard_map/all_to_all | solution.py:122
  424.8 14.1 %gather_fusion.5 = f32[4096,6]{1,0:T(8,128)} fusion(f32[6,2048]{0,1:T(8,128)S(1)} %bitcast.736, s32[4096]{0:T(1024)S(1)} %bitcast_clamp_fusion), kind=kCustom, calls=%fused_computation.6.clone | custom fusion | bytes 212992 | tf_op jit(solution)/shard_map/jit(_take)/gather | solution.py:146
  443.1 23.0 %scatter_custom_fusion.6 = f32[2048,6]{1,0:T(8,128)S(1)} fusion(s32[4096]{0:T(1024)} %bitcast.864, f32[4096,6]{1,0:T(8,128)S(1)} %bitcast.749, f32[]{:T(128)} %constant.7.clone.1), kind=kCustom, calls=%fused_computation.25 | custom fusion | flops 24576 | bytes 49664 | tf_op jit(solution)/shard_map/scatter-add | solution.py:140
  467.8 12.0 %all_to_all.87 = f32[32,1,384]{2,1,0:T(1,128)S(1)} all-to-all(f32[32,1,384]{2,1,0:T(1,128)S(1)} %reshape.2717), channel_id=1, replica_groups=mesh['z'=16,'x'=8,'c'=1,'y'=4] {'x','c','y'}, dimensions={0} | all-to-all | bytes 98304 | tf_op jit(solution)/shard_map/all_to_all | solution.py:121
  499.2 11.6 %scatter_custom_fusion.7 = f32[257,6]{1,0:T(8,128)S(1)} fusion(s32[2048]{0:T(1024)} %bitcast.868, f32[2048,6]{1,0:T(8,128)S(1)} %copy.885, f32[]{:T(128)} %constant.7.clone.1), kind=kCustom, calls=%fused_computation.46 | custom fusion | flops 12288 | bytes 6680 | tf_op jit(solution)/shard_map/scatter-add | solution.py:110
  520.8 11.9 %all_to_all.88 = f32[32,1,384]{2,1,0:T(1,128)S(1)} all-to-all(f32[32,1,384]{2,1,0:T(1,128)S(1)} %reshape.2721), channel_id=1, replica_groups=mesh['z'=16,'x'=8,'c'=1,'y'=4] {'x','c','y'}, dimensions={0} | all-to-all | bytes 98304 | tf_op jit(solution)/shard_map/all_to_all | solution.py:121
  534.1 14.1 %all_to_all.89 = f32[16,1,768]{2,1,0:T(1,128)S(1)} all-to-all(f32[16,1,768]{2,1,0:T(1,128)S(1)} %reshape.2723), channel_id=1, replica_groups=mesh['z'=16,'x'=8,'c'=1,'y'=4] {'z'}, dimensions={0} | all-to-all | bytes 98304 | tf_op jit(solution)/shard_map/all_to_all | solution.py:122
  550.1 14.1 %gather_fusion.7 = f32[4096,6]{1,0:T(8,128)} fusion(f32[6,2048]{0,1:T(8,128)S(1)} %bitcast.733, s32[4096]{0:T(1024)S(1)} %bitcast_clamp_fusion), kind=kCustom, calls=%fused_computation.7.clone | custom fusion | bytes 212992 | tf_op jit(solution)/shard_map/jit(_take)/gather | solution.py:146
  (519 shorter events, 205.1 us)
Async XLA Ops:
  64.8 32.0 %all-to-all-start.1 = ((f32[16,1,6272]{2,1,0:T(1,128)}), f32[16,1,6272]{2,1,0:T(1,128)S(1)}, u32[]{:S(2)}, u32[]{:S(2)}) async-start(f32[16,1,6272]{2,1,0:T(1,128)} %reshape.2695), calls=%async_computation.1 | async-start | bytes 802816 | tf_op jit(solution)/shard_map/all_to_all | solution.py:122
  108.8 23.3 %copy-start.80 = (pred[4,4,128]{2,1,0:T(4,128)(4,1)}, pred[4,4,128]{2,1,0:T(4,128)(4,1)S(1)}, u32[]{:S(2)}) copy-start(pred[4,4,128]{2,1,0:T(4,128)(4,1)S(1)} %get-tuple-element.189) | copy-start | bytes 6148
  108.8 23.3 %copy-start.84 = (pred[4,4,128]{2,1,0:T(4,128)(4,1)}, pred[4,4,128]{2,1,0:T(4,128)(4,1)S(1)}, u32[]{:S(2)}) copy-start(pred[4,4,128]{2,1,0:T(4,128)(4,1)S(1)} %get-tuple-element.190) | copy-start | bytes 6148
  112.0 19.8 %copy-start.112 = (s32[2048,1]{0,1:T(1,128)}, s32[2048,1]{0,1:T(1,128)S(1)}, u32[]{:S(2)}) copy-start(s32[2048,1]{0,1:T(1,128)S(1)} %compare_select_fusion) | copy-start | bytes 24580
  132.6 26.9 %copy-start.10 = (s32[4,1024]{1,0:T(4,128)S(1)}, s32[4,1024]{1,0:T(4,128)}, u32[]{:S(2)}) copy-start(s32[4,1024]{1,0:T(4,128)} %param.14) | copy-start | bytes 49156
  134.1 17.7 %all-to-all-start.2 = ((f32[32,1,384]{2,1,0:T(1,128)}), f32[32,1,384]{2,1,0:T(1,128)S(1)}, u32[]{:S(2)}, u32[]{:S(2)}) async-start(f32[32,1,384]{2,1,0:T(1,128)} %reshape.2697), calls=%async_computation.2 | async-start | bytes 98304 | tf_op jit(solution)/shard_map/all_to_all | solution.py:121
  153.9 17.2 %all-to-all-start.3 = ((f32[16,1,768]{2,1,0:T(1,128)}), f32[16,1,768]{2,1,0:T(1,128)S(1)}, u32[]{:S(2)}, u32[]{:S(2)}) async-start(f32[16,1,768]{2,1,0:T(1,128)} %reshape.2699), calls=%async_computation.3 | async-start | bytes 98304 | tf_op jit(solution)/shard_map/all_to_all | solution.py:122
  159.5 27.5 %copy-start.15 = (pred[4,1024]{1,0:T(4,128)(4,1)}, pred[4,1024]{1,0:T(4,128)(4,1)S(1)}, u32[]{:S(2)}) copy-start(pred[4,1024]{1,0:T(4,128)(4,1)S(1)} %compare_and_fusion) | copy-start | bytes 12292
  214.1 19.6 %copy-start.20 = (f32[6,6]{1,0:T(8,128)S(1)}, f32[6,6]{1,0:T(8,128)}, u32[]{:S(2)}) copy-start(f32[6,6]{1,0:T(8,128)} %fusion.21) | copy-start | bytes 436
  214.1 19.6 %copy-start.24 = (f32[6,256]{1,0:T(8,128)S(1)}, f32[6,256]{1,0:T(8,128)}, u32[]{:S(2)}) copy-start(f32[6,256]{1,0:T(8,128)} %copy-done.23) | copy-start | bytes 18436
  230.0 15.2 %all-to-all-start.5 = ((f32[16,1,768]{2,1,0:T(1,128)}), f32[16,1,768]{2,1,0:T(1,128)S(1)}, u32[]{:S(2)}, u32[]{:S(2)}) async-start(f32[16,1,768]{2,1,0:T(1,128)} %reshape.2703), calls=%async_computation.5 | async-start | bytes 98304 | tf_op jit(solution)/shard_map/all_to_all | solution.py:122
  246.8 21.6 %copy-start.81 = (pred[4,4,128]{2,1,0:T(4,128)(4,1)S(1)}, pred[4,4,128]{2,1,0:T(4,128)(4,1)}, u32[]{:S(2)}) copy-start(pred[4,4,128]{2,1,0:T(4,128)(4,1)} %copy-done.80) | copy-start | bytes 6148
  246.9 21.6 %copy-start.85 = (pred[4,4,128]{2,1,0:T(4,128)(4,1)S(1)}, pred[4,4,128]{2,1,0:T(4,128)(4,1)}, u32[]{:S(2)}) copy-start(pred[4,4,128]{2,1,0:T(4,128)(4,1)} %copy-done.84) | copy-start | bytes 6148
  282.7 30.4 %copy-start.16 = (pred[4,1024]{1,0:T(4,128)(4,1)S(1)}, pred[4,1024]{1,0:T(4,128)(4,1)}, u32[]{:S(2)}) copy-start(pred[4,1024]{1,0:T(4,128)(4,1)} %copy-done.15) | copy-start | bytes 12292
  340.1 19.3 %copy-start.14 = (f32[6,256]{1,0:T(8,128)S(1)}, f32[6,256]{1,0:T(8,128)}, u32[]{:S(2)}) copy-start(f32[6,256]{1,0:T(8,128)} %copy-done.13) | copy-start | bytes 18436
  340.1 19.3 %copy-start.21 = (f32[6,6]{1,0:T(8,128)S(1)}, f32[6,6]{1,0:T(8,128)}, u32[]{:S(2)}) copy-start(f32[6,6]{1,0:T(8,128)} %fusion.21) | copy-start | bytes 436
  355.9 15.0 %all-to-all-start.9 = ((f32[16,1,768]{2,1,0:T(1,128)}), f32[16,1,768]{2,1,0:T(1,128)S(1)}, u32[]{:S(2)}, u32[]{:S(2)}) async-start(f32[16,1,768]{2,1,0:T(1,128)} %reshape.2711), calls=%async_computation.9 | async-start | bytes 98304 | tf_op jit(solution)/shard_map/all_to_all | solution.py:122
  372.5 21.5 %copy-start.82 = (pred[4,4,128]{2,1,0:T(4,128)(4,1)S(1)}, pred[4,4,128]{2,1,0:T(4,128)(4,1)}, u32[]{:S(2)}) copy-start(pred[4,4,128]{2,1,0:T(4,128)(4,1)} %copy-done.80) | copy-start | bytes 6148
  372.5 21.5 %copy-start.86 = (pred[4,4,128]{2,1,0:T(4,128)(4,1)S(1)}, pred[4,4,128]{2,1,0:T(4,128)(4,1)}, u32[]{:S(2)}) copy-start(pred[4,4,128]{2,1,0:T(4,128)(4,1)} %copy-done.84) | copy-start | bytes 6148
  408.3 30.5 %copy-start.17 = (pred[4,1024]{1,0:T(4,128)(4,1)S(1)}, pred[4,1024]{1,0:T(4,128)(4,1)}, u32[]{:S(2)}) copy-start(pred[4,1024]{1,0:T(4,128)(4,1)} %copy-done.15) | copy-start | bytes 12292
  481.8 15.0 %all-to-all-start.13 = ((f32[16,1,768]{2,1,0:T(1,128)}), f32[16,1,768]{2,1,0:T(1,128)S(1)}, u32[]{:S(2)}, u32[]{:S(2)}) async-start(f32[16,1,768]{2,1,0:T(1,128)} %reshape.2719), calls=%async_computation.13 | async-start | bytes 98304 | tf_op jit(solution)/shard_map/all_to_all | solution.py:122
  498.4 20.9 %copy-start.83 = (pred[4,4,128]{2,1,0:T(4,128)(4,1)S(1)}, pred[4,4,128]{2,1,0:T(4,128)(4,1)}, u32[]{:S(2)}) copy-start(pred[4,4,128]{2,1,0:T(4,128)(4,1)} %copy-done.80) | copy-start | bytes 6148
  498.4 20.9 %copy-start.87 = (pred[4,4,128]{2,1,0:T(4,128)(4,1)S(1)}, pred[4,4,128]{2,1,0:T(4,128)(4,1)}, u32[]{:S(2)}) copy-start(pred[4,4,128]{2,1,0:T(4,128)(4,1)} %copy-done.84) | copy-start | bytes 6148
  533.7 30.5 %copy-start.18 = (pred[4,1024]{1,0:T(4,128)(4,1)S(1)}, pred[4,1024]{1,0:T(4,128)(4,1)}, u32[]{:S(2)}) copy-start(pred[4,1024]{1,0:T(4,128)(4,1)} %copy-done.15) | copy-start | bytes 12292
  (98 other events, 1089.6 us)
